TPU v7x, 32 devices: a whole 2x2x4 slice. The times are simulated.
32 devices in a mesh: clips: 2 (over y), space: 8 (over z, x), tm: 2 (over core).
Axes of the slice: x: 2, y: 2, z: 4, core: 2. Of those that a mesh axis runs over, the one named last changes fastest.
Arguments:
- frames: bfloat16 [2, 2, 16, 112, 192], P('clips', 'tm', 'space'), parts along dimension 0, may hold values from -100 to 100
- norm1_gain: float32 [192], replicated, may hold values from 0.1 to 1.9
- conv1_weight: bfloat16 [3, 3, 3, 192, 192], replicated, may hold values from -0.078125 to 0.078125
- conv1_bias: float32 [192], replicated, may hold values from -3 to 3
- norm2_gain: float32 [192], replicated, may hold values from 0.1 to 1.9
- conv2_weight: bfloat16 [3, 3, 3, 192, 192], replicated, may hold values from -0.078125 to 0.078125
- conv2_bias: float32 [192], replicated, may hold values from -3 to 3
- attn_gain: float32 [192], replicated, may hold values from 0.5 to 3
- w_query: bfloat16 [192, 192], replicated, may hold values from -3 to 3
- b_query: float32 [192], replicated, may hold values from -4 to 4
- w_key: bfloat16 [192, 192], replicated, may hold values from -1 to 2
- w_value: bfloat16 [192, 192], replicated, may hold values from -0.4375 to 0.4375
- b_value: float32 [192], replicated, may hold values from -3 to 3
- w_out: bfloat16 [192, 192], replicated, may hold values from -0.4375 to 0.4375
- b_out: float32 [192], replicated, may hold values from -3 to 3
Outputs:
- decoded: float32 [2, 2, 16, 112, 192], P('clips', 'tm', 'space'), parts along dimension 0
There are 2 independent parts, one for each index of `clips`. A program takes and returns all parts, laid end to end along the dimension named above; an argument that names none is the same for every part. Nothing has to cross between parts.
All inputs are finite; a program needn't handle non-finite values.
Results may differ from a plain program's by a relative error of at most 0.02.
Values may be sent and summed in bfloat16 or wider, within the bound.
No kernel may reach another device: no remote copies, remote signals or barrier semaphores. Data moves between devices by JAX's collectives and lax.ppermute only.
A program may use at most 128 MiB of HBM per device.

v0:
```python
import math
import jax
import jax.numpy as jnp
from jax import lax
from jax.sharding import PartitionSpec as P

epsilon = 1e-06


def shifted(block, axis, distance):
    devices = range(lax.axis_size(axis))
    route = [((i - distance) % len(devices), i) for i in devices]
    return lax.ppermute(block, axis, route)


def extended(value, sides, width):
    for axis, dim in sides:
        size, length = (lax.axis_size(axis), value.shape[dim])
        up = [(i, (i + 1) % size) for i in range(size - 1)]
        down = [(j, i) for i, j in up]
        last = lax.slice_in_dim(value, length - width, length, axis=dim)
        first = lax.slice_in_dim(value, 0, width, axis=dim)
        before = lax.ppermute(last, axis, up)
        after = lax.ppermute(first, axis, down)
        value = jnp.concatenate([before, value, after], axis=dim)
    return value


def rms_scale(values, gain):
    return values * lax.rsqrt(jnp.mean(values * values, axis=-1, keepdims=True) + epsilon) * gain


def causal_conv(inputs, weight, bias):
    frame_count, row_count, col_count, channels = inputs.shape
    is_first = lax.axis_index("tm") == 0
    remote = shifted(inputs, "tm", 1)
    earlier = jnp.concatenate([jnp.zeros_like(remote), remote[:-1]], axis=0)
    previous = jnp.where(is_first, earlier, remote)
    paired = extended(jnp.stack([inputs, previous]), (("space", 2),), 1)
    current = paired[0]
    previous = paired[1]
    oldest = jnp.concatenate([jnp.zeros_like(current), current[:-1]], axis=0)
    tap_list = []
    for source in (oldest, previous, current):
        widened = jnp.pad(source, ((0, 0), (0, 0), (1, 1), (0, 0)))
        for row_off in range(3):
            for col_off in range(3):
                tap_list.append(
                    widened[:, row_off : row_off + row_count, col_off : col_off + col_count, :]
                )
    patches = jnp.concatenate(tap_list, axis=-1).reshape(
        frame_count * row_count * col_count, 27 * channels
    )
    summed = jnp.dot(
        patches, weight.reshape(27 * channels, channels), preferred_element_type=jnp.float32
    )
    return summed.reshape(frame_count, row_count, col_count, channels) + bias


def absorb(running, queries, key_rows):
    top_old, total_old, accum = running
    scores = jnp.einsum("fqc,fkc->fqk", queries, key_rows, preferred_element_type=jnp.float32)
    top_new = jnp.maximum(top_old, jnp.max(scores, axis=-1))
    weights = jnp.exp(scores - top_new[..., None])
    total_new = jnp.sum(weights, axis=-1)
    accum = jnp.einsum(
        "fqk,fkc->fqc", weights.astype(jnp.bfloat16), key_rows, preferred_element_type=jnp.float32
    )
    return (top_new, total_new, accum)


def local(
    frames,
    norm1_gain,
    conv1_weight,
    conv1_bias,
    norm2_gain,
    conv2_weight,
    conv2_bias,
    attn_gain,
    w_query,
    b_query,
    w_key,
    w_value,
    b_value,
    w_out,
    b_out,
):
    local_frames = frames[:, 0]
    frame_count, row_count, col_count, channels = local_frames.shape
    frame_values = local_frames.astype(jnp.float32)
    first_act = jax.nn.silu(rms_scale(frame_values, norm1_gain)).astype(jnp.bfloat16)
    first_out = causal_conv(first_act, conv1_weight, conv1_bias)
    second_act = jax.nn.silu(rms_scale(first_out, norm2_gain)).astype(jnp.bfloat16)
    second_out = causal_conv(second_act, conv2_weight, conv2_bias)
    residual = frame_values + second_out
    normed = rms_scale(residual, attn_gain).astype(jnp.bfloat16)
    token_count = row_count * col_count
    flat = normed.reshape(frame_count * token_count, channels)
    query = (jnp.dot(flat, w_query, preferred_element_type=jnp.float32) + b_query).astype(
        jnp.bfloat16
    )
    folded = (
        jnp.dot(query, w_key.T, preferred_element_type=jnp.float32) * (1.0 / math.sqrt(channels))
    ).astype(jnp.bfloat16)
    folded = folded.reshape(frame_count, token_count, channels)
    initial = (
        jnp.full((frame_count, token_count), -1e30, jnp.float32),
        jnp.zeros((frame_count, token_count), jnp.float32),
        jnp.zeros((frame_count, token_count, channels), jnp.float32),
    )
    slot_queries = folded

    def absorb_one(running, received, offset, slot_queries=slot_queries):
        return absorb(running, slot_queries, received.reshape(1, -1, channels))

    start_state = tuple((item for item in initial))
    results = [
        absorb_one(
            start_state, lax.all_gather(normed[0], "space", axis=0, tiled=True), jnp.int32(0)
        )
    ]
    total = jnp.concatenate([item[1] for item in results], axis=0)
    accum = jnp.concatenate([item[2] for item in results], axis=0)
    mixed = (accum / total[..., None]).astype(jnp.bfloat16).reshape(-1, channels)
    value = (jnp.dot(mixed, w_value, preferred_element_type=jnp.float32) + b_value).astype(
        jnp.bfloat16
    )
    decoded = (
        residual.reshape(-1, channels)
        + jnp.dot(value, w_out, preferred_element_type=jnp.float32)
        + b_out
    )
    return decoded.reshape(frame_count, 1, row_count, col_count, channels)


def solution(mesh):
    placed = (
        P("clips", "tm", "space", None, None),
        P(),
        P(),
        P(),
        P(),
        P(),
        P(),
        P(),
        P(),
        P(),
        P(),
        P(),
        P(),
        P(),
        P(),
    )
    return jax.shard_map(
        local,
        mesh=mesh,
        in_specs=placed,
        out_specs=P("clips", "tm", "space", None, None),
        check_vma=False,
    )
```

profile of v0, /device:TPU:0, one launch (start us, length us, event | category | flops | bytes accessed | tf_op | source)
XLA Modules:
  0.0 90.7 jit_solution(12605600663512206442)
XLA Ops:
  0.0 1.1 %copy.31 = bf16[1,1,2,112,192]{4,3,2,1,0:T(8,128)(2,1)S(1)} copy(bf16[1,1,2,112,192]{3,4,2,1,0:T(8,128)(2,1)} %param.15) | data formatting | bytes 172032 | tf_op args[0]
  1.3 0.8 fusion.31
  3.7 4.8 %collective-permute-start.1 = (bf16[2,1,1,112,192]{4,3,2,1,0:T(8,128)(2,1)S(1)}, bf16[2,1,1,112,192]{4,3,2,1,0:T(8,128)(2,1)S(1)}, u32[]{:S(2)}, u32[]{:S(2)}) collective-permute-start(bf16[2,1,1,112,192]{4,3,2,1,0:T(8,128)(2,1)S(1)} %get-tuple-element.47), channel_id=1, source_target_pairs={{0,2},{2,4},{4,6},{6,8},{8,10},{10,12},{12,14},{1,3},{3,5},{5,7},{... | collective-permute-start | bytes 258056 | tf_op jit(solution)/shard_map/ppermute | solution.py:23
  8.4 1.3 %collective-permute-start.2 = (bf16[2,1,1,112,192]{4,3,2,1,0:T(8,128)(2,1)S(1)}, bf16[2,1,1,112,192]{4,3,2,1,0:T(8,128)(2,1)S(1)}, u32[]{:S(2)}, u32[]{:S(2)}) collective-permute-start(bf16[2,1,1,112,192]{4,3,2,1,0:T(8,128)(2,1)S(1)} %get-tuple-element.48), channel_id=1, source_target_pairs={{2,0},{4,2},{6,4},{8,6},{10,8},{12,10},{14,12},{3,1},{5,3},{7,5},{... | collective-permute-start | bytes 258056 | tf_op jit(solution)/shard_map/ppermute | solution.py:24
  9.8 1.3 %collective-permute-done.1 = bf16[2,1,1,112,192]{4,3,2,1,0:T(8,128)(2,1)S(1)} collective-permute-done((bf16[2,1,1,112,192]{4,3,2,1,0:T(8,128)(2,1)S(1)}, bf16[2,1,1,112,192]{4,3,2,1,0:T(8,128)(2,1)S(1)}, u32[]{:S(2)}, u32[]{:S(2)}) %collective-permute-start.1) | collective-permute-done | bytes 86048 | tf_op jit(solution)/shard_map/ppermute | solution.py:23
  11.1 4.1 %collective-permute-done.2 = bf16[2,1,1,112,192]{4,3,2,1,0:T(8,128)(2,1)S(1)} collective-permute-done((bf16[2,1,1,112,192]{4,3,2,1,0:T(8,128)(2,1)S(1)}, bf16[2,1,1,112,192]{4,3,2,1,0:T(8,128)(2,1)S(1)}, u32[]{:S(2)}, u32[]{:S(2)}) %collective-permute-start.2) | collective-permute-done | bytes 86048 | tf_op jit(solution)/shard_map/ppermute | solution.py:24
  15.4 1.2 %pad_slice_fusion.16 = (bf16[1,2,112,192]{3,2,1,0:T(8,128)(2,1)S(1)}, bf16[1,2,112,192]{3,2,1,0:T(8,128)(2,1)S(1)}, bf16[1,2,112,192]{3,2,1,0:T(8,128)(2,1)S(1)}...) fusion(bf16[1,4,112,192]{3,2,1,0:T(8,128)(2,1)S(1)} %get-tuple-, ...), kind=kLoop, calls=%fused_computation.67 | loop fusion | bytes 2695168 | tf_op jit(solution)/shard_map/slice | solution.py:49
  16.8 5.4 %concatenate.13 = bf16[1,2,112,5184]{3,2,1,0:T(8,128)(2,1)} concatenate(bf16[1,2,112,192]{3,2,1,0:T(8,128)(2,1)S(1)} %pad.24, bf16[1,2,112,192]{3,2,1,0:T(8,128)(2,1)S(1)} %pad.25, bf16[1,2,112,192]{3,2,1,0:T(8,128)(2,1)S(1)} %pad.26, bf16[1,2,112,192]{3,2,1,0:T(8,128)(2,1)S(1)} %pad.24, bf16[1,2,112,192]{3,2,1,0:T(8,128)(2,1)S(1)} %pad.25, bf16[1,2,112,192]{3,2,1,0:T(8,128)(2,1)S(1)} %pad.26, ...), dimensions={3} | concatenate | bytes 4644864 | tf_op jit(solution)/shard_map/concatenate | solution.py:51
  22.3 2.5 %multiply_reduce_fusion.1 = (f32[2,112]{1,0:T(2,128)S(1)}, f32[2,112,192]{2,1,0:T(8,128)S(1)}) fusion(f32[192]{0:T(256)S(1)} %copy-done.7, bf16[5184,192,1]{1,0,2:T(8,128)(2,1)S(1)} %bitcast.83, bf16[1,2,112,5184]{3,2,1,0:T(8,128)(2,1)} %concatenate.13), kind=kOutput, calls=%fused_computation.54 | convolution fusion | flops 446035744 | bytes 4486784 | tf_op jit(solution)/shard_map/dot_general | solution.py:54
  25.2 1.2 %collective-permute-done.3 = bf16[1,2,112,192]{3,2,1,0:T(8,128)(2,1)S(1)} collective-permute-done((bf16[1,2,112,192]{3,2,1,0:T(8,128)(2,1)S(1)}, bf16[1,2,112,192]{3,2,1,0:T(8,128)(2,1)S(1)}, u32[]{:S(2)}, u32[]{:S(2)}) %collective-permute-start.3) | collective-permute-done | bytes 86048 | tf_op jit(solution)/shard_map/ppermute | solution.py:13
  26.4 4.4 %collective-permute-start.4 = (bf16[2,1,1,112,192]{4,3,2,1,0:T(8,128)(2,1)S(1)}, bf16[2,1,1,112,192]{4,3,2,1,0:T(8,128)(2,1)S(1)}, u32[]{:S(2)}, u32[]{:S(2)}) collective-permute-start(bf16[2,1,1,112,192]{4,3,2,1,0:T(8,128)(2,1)S(1)} %get-tuple-element.27), channel_id=1, source_target_pairs={{0,2},{2,4},{4,6},{6,8},{8,10},{10,12},{12,14},{1,3},{3,5},{5,7},{... | collective-permute-start | bytes 258056 | tf_op jit(solution)/shard_map/ppermute | solution.py:23
  30.8 1.3 %collective-permute-start.5 = (bf16[2,1,1,112,192]{4,3,2,1,0:T(8,128)(2,1)S(1)}, bf16[2,1,1,112,192]{4,3,2,1,0:T(8,128)(2,1)S(1)}, u32[]{:S(2)}, u32[]{:S(2)}) collective-permute-start(bf16[2,1,1,112,192]{4,3,2,1,0:T(8,128)(2,1)S(1)} %get-tuple-element.28), channel_id=1, source_target_pairs={{2,0},{4,2},{6,4},{8,6},{10,8},{12,10},{14,12},{3,1},{5,3},{7,5},{... | collective-permute-start | bytes 258056 | tf_op jit(solution)/shard_map/ppermute | solution.py:24
  32.1 1.4 %collective-permute-done.4 = bf16[2,1,1,112,192]{4,3,2,1,0:T(8,128)(2,1)S(1)} collective-permute-done((bf16[2,1,1,112,192]{4,3,2,1,0:T(8,128)(2,1)S(1)}, bf16[2,1,1,112,192]{4,3,2,1,0:T(8,128)(2,1)S(1)}, u32[]{:S(2)}, u32[]{:S(2)}) %collective-permute-start.4) | collective-permute-done | bytes 86048 | tf_op jit(solution)/shard_map/ppermute | solution.py:23
  33.5 4.1 %collective-permute-done.5 = bf16[2,1,1,112,192]{4,3,2,1,0:T(8,128)(2,1)S(1)} collective-permute-done((bf16[2,1,1,112,192]{4,3,2,1,0:T(8,128)(2,1)S(1)}, bf16[2,1,1,112,192]{4,3,2,1,0:T(8,128)(2,1)S(1)}, u32[]{:S(2)}, u32[]{:S(2)}) %collective-permute-start.5) | collective-permute-done | bytes 86048 | tf_op jit(solution)/shard_map/ppermute | solution.py:24
  37.8 0.9 %pad_slice_fusion.4 = (bf16[1,2,112,192]{3,2,1,0:T(8,128)(2,1)S(1)}, bf16[1,2,112,192]{3,2,1,0:T(8,128)(2,1)S(1)}, bf16[1,2,112,192]{3,2,1,0:T(8,128)(2,1)S(1)},...) fusion(bf16[1,4,112,192]{3,2,1,0:T(8,128)(2,1)S(1)} %get-tuple-, ...), kind=kLoop, calls=%fused_computation.55 | loop fusion | bytes 1347584 | tf_op jit(solution)/shard_map/slice | solution.py:49
  38.7 1.0 %pad_slice_fusion.10 = (bf16[1,2,112,192]{3,2,1,0:T(8,128)(2,1)}, bf16[1,2,112,192]{3,2,1,0:T(8,128)(2,1)}, bf16[1,2,112,192]{3,2,1,0:T(8,128)(2,1)}, bf16[1,2,1...) fusion(bf16[1,4,112,192]{3,2,1,0:T(8,128)(2,1)S(1)} %get-tuple-, ...), kind=kLoop, calls=%fused_computation.61 | loop fusion | bytes 1347584 | tf_op jit(solution)/shard_map/slice | solution.py:49
  39.7 5.4 %concatenate.15 = bf16[1,2,112,5184]{3,2,1,0:T(8,128)(2,1)} concatenate(bf16[1,2,112,192]{3,2,1,0:T(8,128)(2,1)S(1)} %pad.24, bf16[1,2,112,192]{3,2,1,0:T(8,128)(2,1)S(1)} %pad.25, bf16[1,2,112,192]{3,2,1,0:T(8,128)(2,1)S(1)} %pad.26, bf16[1,2,112,192]{3,2,1,0:T(8,128)(2,1)S(1)} %pad.24, bf16[1,2,112,192]{3,2,1,0:T(8,128)(2,1)S(1)} %pad.25, bf16[1,2,112,192]{3,2,1,0:T(8,128)(2,1)S(1)} %pad.26, ...), dimensions={3} | concatenate | bytes 4644864 | tf_op jit(solution)/shard_map/concatenate | solution.py:51
  45.1 3.3 %multiply_reduce_fusion = (f32[2,112]{1,0:T(2,128)S(1)}, f32[2,112,192]{2,1,0:T(8,128)S(1)}) fusion(f32[192]{0:T(256)S(1)} %copy-done.8, bf16[5184,192,1]{1,0,2:T(8,128)(2,1)} %bitcast.86, bf16[1,2,112,5184]{3,2,1,0:T(8,128)(2,1)} %concatenate.15, bf16[1,1,2,112,192]{4,3,2,1,0:T(8,128)(2,1)S(1)} %copy.31), kind=kOutput, calls=%fused_computation.52 | convolution fusion | flops 446121760 | bytes 4572800 | tf_op jit(solution)/shard_map/dot_general | solution.py:54
  49.5 32.1 %all_gather.3 = bf16[16,112,192]{1,2,0:T(8,128)(2,1)S(1)} all-gather(bf16[2,112,192]{1,2,0:T(8,128)(2,1)S(1)} %copy.36), channel_id=1, replica_groups=mesh['clips'=2,'space'=8,'tm'=2] {'space'}, dimensions={0}, use_global_device_ids=true | all-gather | bytes 774144 | tf_op jit(solution)/shard_map/all_gather | solution.py:120
  82.0 1.8 %reshape.197 = bf16[1792,192]{0,1:T(8,128)(2,1)} reshape(bf16[16,112,192]{1,0,2:T(8,128)(2,1)S(1)} %copy.37) | data formatting | bytes 1376256 | tf_op jit(solution)/shard_map/reshape.9
  83.9 1.4 %fusion.19 = bf16[224,192]{0,1:T(8,128)(2,1)S(1)} fusion(bf16[192,192]{1,0:T(8,128)(2,1)} %param.25, bf16[224,192]{1,0:T(8,128)(2,1)S(1)} %bitcast.84, bf16[192,192]{1,0:T(8,128)(2,1)} %param.23, f32[192]{0:T(256)} %param.24), kind=kOutput, calls=%fused_computation.19 | convolution fusion | flops 33202176 | bytes 320256 | tf_op jit(solution)/shard_map/dot_general | solution.py:104
  85.3 1.6 %fusion.43 = (f32[224]{0:T(256)S(1)}, f32[224,1792]{1,0:T(8,128)S(1)}) fusion(bf16[224,192]{0,1:T(8,128)(2,1)S(1)} %fusion.19, bf16[1792,192]{0,1:T(8,128)(2,1)} %reshape.197), kind=kOutput, calls=%fused_computation.93 | convolution fusion | flops 154541856 | bytes 2380672 | tf_op jit(solution)/shard_map/fqc,fkc->fqk/dot_general | solution.py:62
  87.3 1.1 %fusion.17 = bf16[224,192]{0,1:T(8,128)(2,1)} fusion(bf16[1792,192]{0,1:T(8,128)(2,1)S(1)} %copy-done.1, f32[224,1792]{1,0:T(8,128)S(1)} %get-tuple-element.56, f32[224]{0:T(256)S(1)} %broadcast_maximum_fusion, f32[224]{0:T(256)S(1)} %fusion.4), kind=kOutput, calls=%fused_computation.17 | convolution fusion | flops 155029504 | bytes 2381568 | tf_op jit(solution)/shard_map/fqk,fkc->fqc/dot_general | solution.py:66
  88.4 1.4 %fusion.15 = f32[224,192]{0,1:T(8,128)S(1)} fusion(f32[224,192]{0,1:T(8,128)S(1)} %copy-done.2, bf16[192,192]{1,0:T(8,128)(2,1)} %param.28, bf16[224,192]{0,1:T(8,128)(2,1)} %fusion.17, bf16[192,192]{1,0:T(8,128)(2,1)} %param.26, f32[192]{0:T(256)S(1)} %copy-done.5, f32[192]{0:T(256)S(1)} %copy-done.6), kind=kOutput, calls=%fused_computation.12 | convolution fusion | flops 33202176 | bytes 579072 | tf_op jit(solution)/shard_map/dot_general | solution.py:131
  (49 shorter events, 5.4 us)
Async XLA Ops:
  0.0 22.2 %copy-start = (bf16[3,3,3,192,192]{4,3,2,1,0:T(8,128)(2,1)S(1)}, bf16[3,3,3,192,192]{4,3,2,1,0:T(8,128)(2,1)}, u32[]{:S(2)}) copy-start(bf16[3,3,3,192,192]{4,3,2,1,0:T(8,128)(2,1)} %param.17) | copy-start | bytes 5971972
  2.1 1.5 %collective-permute-start = (bf16[1,2,112,192]{3,2,1,0:T(8,128)(2,1)S(1)}, bf16[1,2,112,192]{3,2,1,0:T(8,128)(2,1)S(1)}, u32[]{:S(2)}, u32[]{:S(2)}) collective-permute-start(bf16[1,2,112,192]{3,2,1,0:T(8,128)(2,1)S(1)} %fusion.31), channel_id=1, source_target_pairs={{1,0},{0,1},{3,2},{2,3},{5,4},{4,5},{7,6},{6,7},{9,8},{8,9},{11,10... | collective-permute-start | bytes 258056 | tf_op jit(solution)/shard_map/ppermute | solution.py:13
  3.7 7.5 %collective-permute-start.1 = (bf16[2,1,1,112,192]{4,3,2,1,0:T(8,128)(2,1)S(1)}, bf16[2,1,1,112,192]{4,3,2,1,0:T(8,128)(2,1)S(1)}, u32[]{:S(2)}, u32[]{:S(2)}) collective-permute-start(bf16[2,1,1,112,192]{4,3,2,1,0:T(8,128)(2,1)S(1)} %get-tuple-element.47), channel_id=1, source_target_pairs={{0,2},{2,4},{4,6},{6,8},{8,10},{10,12},{12,14},{1,3},{3,5},{5,7},{... | collective-permute-start | bytes 258056 | tf_op jit(solution)/shard_map/ppermute | solution.py:23
  8.4 6.8 %collective-permute-start.2 = (bf16[2,1,1,112,192]{4,3,2,1,0:T(8,128)(2,1)S(1)}, bf16[2,1,1,112,192]{4,3,2,1,0:T(8,128)(2,1)S(1)}, u32[]{:S(2)}, u32[]{:S(2)}) collective-permute-start(bf16[2,1,1,112,192]{4,3,2,1,0:T(8,128)(2,1)S(1)} %get-tuple-element.48), channel_id=1, source_target_pairs={{2,0},{4,2},{6,4},{8,6},{10,8},{12,10},{14,12},{3,1},{5,3},{7,5},{... | collective-permute-start | bytes 258056 | tf_op jit(solution)/shard_map/ppermute | solution.py:24
  16.8 5.4 %copy-start.7 = (f32[192]{0:T(256)S(1)}, f32[192]{0:T(256)}, u32[]{:S(2)}) copy-start(f32[192]{0:T(256)} %param.18) | copy-start | bytes 2308
  22.3 2.6 %copy-start.3 = (f32[192]{0:T(256)S(1)}, f32[192]{0:T(256)}, u32[]{:S(2)}) copy-start(f32[192]{0:T(256)} %param.19) | copy-start | bytes 2308
  25.0 1.4 %collective-permute-start.3 = (bf16[1,2,112,192]{3,2,1,0:T(8,128)(2,1)S(1)}, bf16[1,2,112,192]{3,2,1,0:T(8,128)(2,1)S(1)}, u32[]{:S(2)}, u32[]{:S(2)}) collective-permute-start(bf16[1,2,112,192]{3,2,1,0:T(8,128)(2,1)S(1)} %fusion.55), channel_id=1, source_target_pairs={{1,0},{0,1},{3,2},{2,3},{5,4},{4,5},{7,6},{6,7},{9,8},{8,9},{11,10... | collective-permute-start | bytes 258056 | tf_op jit(solution)/shard_map/ppermute | solution.py:13
  26.4 7.1 %collective-permute-start.4 = (bf16[2,1,1,112,192]{4,3,2,1,0:T(8,128)(2,1)S(1)}, bf16[2,1,1,112,192]{4,3,2,1,0:T(8,128)(2,1)S(1)}, u32[]{:S(2)}, u32[]{:S(2)}) collective-permute-start(bf16[2,1,1,112,192]{4,3,2,1,0:T(8,128)(2,1)S(1)} %get-tuple-element.27), channel_id=1, source_target_pairs={{0,2},{2,4},{4,6},{6,8},{8,10},{10,12},{12,14},{1,3},{3,5},{5,7},{... | collective-permute-start | bytes 258056 | tf_op jit(solution)/shard_map/ppermute | solution.py:23
  30.8 6.8 %collective-permute-start.5 = (bf16[2,1,1,112,192]{4,3,2,1,0:T(8,128)(2,1)S(1)}, bf16[2,1,1,112,192]{4,3,2,1,0:T(8,128)(2,1)S(1)}, u32[]{:S(2)}, u32[]{:S(2)}) collective-permute-start(bf16[2,1,1,112,192]{4,3,2,1,0:T(8,128)(2,1)S(1)} %get-tuple-element.28), channel_id=1, source_target_pairs={{2,0},{4,2},{6,4},{8,6},{10,8},{12,10},{14,12},{3,1},{5,3},{7,5},{... | collective-permute-start | bytes 258056 | tf_op jit(solution)/shard_map/ppermute | solution.py:24
  39.7 5.4 %copy-start.8 = (f32[192]{0:T(256)S(1)}, f32[192]{0:T(256)}, u32[]{:S(2)}) copy-start(f32[192]{0:T(256)} %param.21) | copy-start | bytes 2308
  45.1 3.4 %copy-start.4 = (f32[192]{0:T(256)S(1)}, f32[192]{0:T(256)}, u32[]{:S(2)}) copy-start(f32[192]{0:T(256)} %param.22) | copy-start | bytes 2308
  83.8 3.4 %copy-start.1 = (bf16[1792,192]{0,1:T(8,128)(2,1)S(1)}, bf16[1792,192]{0,1:T(8,128)(2,1)}, u32[]{:S(2)}) copy-start(bf16[1792,192]{0,1:T(8,128)(2,1)} %reshape.197) | copy-start | bytes 2064388
  86.9 1.6 %copy-start.2 = (f32[224,192]{0,1:T(8,128)S(1)}, f32[224,192]{0,1:T(8,128)}, u32[]{:S(2)}) copy-start(f32[224,192]{0,1:T(8,128)} %copy.38) | copy-start | bytes 516100
  86.9 1.6 %copy-start.5 = (f32[192]{0:T(256)S(1)}, f32[192]{0:T(256)}, u32[]{:S(2)}) copy-start(f32[192]{0:T(256)} %param.29) | copy-start | bytes 2308
  86.9 1.5 %copy-start.6 = (f32[192]{0:T(256)S(1)}, f32[192]{0:T(256)}, u32[]{:S(2)}) copy-start(f32[192]{0:T(256)} %param.27) | copy-start | bytes 2308
where the time goes:
time: 91.8 us; the launch traced here: 90.7 us
  blocking collectives  32.1 us (35%)
  local copies, waits for them, and re-layouts  19.6 us (21%)
  starting transfers between devices  12.3 us (13%)
  waiting for transfers between devices  12.2 us (13%)
  matrix products  11.4 us (12%)
  other arithmetic  2.82 us (3%)
    all_gather x1, blocking collectives, local(): lax.all_gather(normed[0], 'space', axis=0, tiled=True)  32.1 us
    concatenate x2, local copies, waits for them, and re-layouts, causal_conv(): jnp.concatenate(tap_list, axis=-1)  10.8 us
    ppermute x2, starting transfers between devices, extended(): before = lax.ppermute(last, axis, up)  9.11 us
    ppermute x2, waiting for transfers between devices, extended(): after = lax.ppermute(first, axis, down)  8.24 us
    dot_general x2, matrix products, causal_conv(): jnp.dot(patches, weight.reshape(27 * channels, channels), preferred_eleme...  5.88 us
    slice x5, local copies, waits for them, and re-layouts, causal_conv(): widened[:, row_off:row_off + row_count, col_off:col_off + col_count, :]  3.21 us
    ppermute x2, waiting for transfers between devices, extended(): before = lax.ppermute(last, axis, up)  2.7 us
    ppermute x2, starting transfers between devices, extended(): after = lax.ppermute(first, axis, down)  2.58 us
  transfers between devices with their start and end apart: 6, of which 6 were waited for; matrix products, arithmetic and copies ran while one was open for 1% of the time, Pallas kernels for 0%

commit v1 on v0

--- a/solution.py
+++ b/solution.py
@@ -5,6 +5,16 @@
 from jax.sharding import PartitionSpec as P
 
 epsilon = 1e-06
+
+
+def collect(x, axis, dim):
+    ways, here, lap = (lax.axis_size(axis), lax.axis_index(axis), x.shape[dim])
+    dims = [n * ways if d == dim else n for d, n in enumerate(x.shape)]
+    full = lax.dynamic_update_slice_in_dim(jnp.zeros(dims, x.dtype), x, here * lap, axis=dim)
+    for far in range(1, ways):
+        x = lax.ppermute(x, axis, [(d, (d + 1) % ways) for d in range(ways)])
+        full = lax.dynamic_update_slice_in_dim(full, x, (here - far) % ways * lap, axis=dim)
+    return full
 
 
 def shifted(block, axis, distance):
@@ -115,11 +125,7 @@
         return absorb(running, slot_queries, received.reshape(1, -1, channels))
 
     start_state = tuple((item for item in initial))
-    results = [
-        absorb_one(
-            start_state, lax.all_gather(normed[0], "space", axis=0, tiled=True), jnp.int32(0)
-        )
-    ]
+    results = [absorb_one(start_state, collect(normed[0], "space", 0), jnp.int32(0))]
     total = jnp.concatenate([item[1] for item in results], axis=0)
     accum = jnp.concatenate([item[2] for item in results], axis=0)
     mixed = (accum / total[..., None]).astype(jnp.bfloat16).reshape(-1, channels)

time: 91.8 us -> 116 us (1.26)
  waiting for transfers between devices: 12.2 us -> 60.4 us
  blocking collectives: 32.1 us -> 0 us
  other arithmetic: 2.82 us -> 6.51 us
  local copies, waits for them, and re-layouts: 19.6 us -> 22 us
  starting transfers between devices: 12.3 us -> 14 us
    ppermute x0 -> x7, waiting for transfers between devices: none -> 47.9 us  [collect(): x = lax.ppermute(x, axis, [(d, (d + 1) % ways) for d in range(ways)])]
    all_gather x1 -> x0, blocking collectives: 32.1 us -> none  [local(): lax.all_gather(normed[0], 'space', axis=0, tiled=True)]
    dynamic_update_slice x0 -> x7, local copies, waits for them, and re-layouts: none -> 4.53 us  [collect(): lax.dynamic_update_slice_in_dim(full, x, (here - far) % ways * lap, axis=...]
    another operation x1 -> x0, local copies, waits for them, and re-layouts: 1.81 us -> none
    ppermute x0 -> x7, starting transfers between devices: none -> 1.73 us  [collect(): x = lax.ppermute(x, axis, [(d, (d + 1) % ways) for d in range(ways)])]
    reduce_sum x1, other arithmetic: 0.37 us -> 1.82 us  [absorb(): total_new = jnp.sum(weights, axis=-1)]
    dot_general x1, matrix products: 1.59 us -> 2.94 us  [absorb(): jnp.einsum('fqc,fkc->fqk', queries, key_rows, preferred_element_type=jnp....]
    dot_general x1, matrix products: 1.4 us -> 0.17 us  [local(): jnp.dot(flat, w_query, preferred_element_type=jnp.float32) + b_query]
  transfers between devices with their start and end apart: 6 -> 13, of which waited for: 6 -> 13; matrix products, arithmetic and copies ran while one was open for 1% -> 5% of each run, Pallas kernels for 0% -> 0%
where the time goes in v1:
time: 116 us; the launch traced here: 115 us
  waiting for transfers between devices  60.4 us (52%)
  local copies, waits for them, and re-layouts  22 us (19%)
  starting transfers between devices  14 us (12%)
  matrix products  11.5 us (10%)
  other arithmetic  6.51 us (6%)
    ppermute x7, waiting for transfers between devices, collect(): x = lax.ppermute(x, axis, [(d, (d + 1) % ways) for d in range(ways)])  47.9 us
    concatenate x2, local copies, waits for them, and re-layouts, causal_conv(): jnp.concatenate(tap_list, axis=-1)  10.9 us
    ppermute x2, starting transfers between devices, extended(): before = lax.ppermute(last, axis, up)  9.1 us
    ppermute x2, waiting for transfers between devices, extended(): after = lax.ppermute(first, axis, down)  8.24 us
    dot_general x2, matrix products, causal_conv(): jnp.dot(patches, weight.reshape(27 * channels, channels), preferred_eleme...  5.92 us
    dynamic_update_slice x7, local copies, waits for them, and re-layouts, collect(): lax.dynamic_update_slice_in_dim(full, x, (here - far) % ways * lap, axis=...  4.53 us
    slice x5, local copies, waits for them, and re-layouts, causal_conv(): widened[:, row_off:row_off + row_count, col_off:col_off + col_count, :]  3.19 us
    dot_general x1, matrix products, absorb(): jnp.einsum('fqc,fkc->fqk', queries, key_rows, preferred_element_type=jnp....  2.94 us
  transfers between devices with their start and end apart: 13, of which 13 were waited for; matrix products, arithmetic and copies ran while one was open for 5% of the time, Pallas kernels for 0%

profile of v1, /device:TPU:0, one launch (start us, length us, event | category | flops | bytes accessed | tf_op | source)
XLA Modules:
  0.0 114.9 jit_solution(10368369135242089654)
XLA Ops:
  3.7 4.8 %collective-permute-start.1 = (bf16[2,1,1,112,192]{4,3,2,1,0:T(8,128)(2,1)S(1)}, bf16[2,1,1,112,192]{4,3,2,1,0:T(8,128)(2,1)S(1)}, u32[]{:S(2)}, u32[]{:S(2)}) collective-permute-start(bf16[2,1,1,112,192]{4,3,2,1,0:T(8,128)(2,1)S(1)} %get-tuple-element.49), channel_id=1, source_target_pairs={{0,2},{2,4},{4,6},{6,8},{8,10},{10,12},{12,14},{1,3},{3,5},{5,7},{... | collective-permute-start | bytes 258056 | tf_op jit(solution)/shard_map/ppermute | solution.py:33
  8.4 1.3 %collective-permute-start.2 = (bf16[2,1,1,112,192]{4,3,2,1,0:T(8,128)(2,1)S(1)}, bf16[2,1,1,112,192]{4,3,2,1,0:T(8,128)(2,1)S(1)}, u32[]{:S(2)}, u32[]{:S(2)}) collective-permute-start(bf16[2,1,1,112,192]{4,3,2,1,0:T(8,128)(2,1)S(1)} %get-tuple-element.50), channel_id=1, source_target_pairs={{2,0},{4,2},{6,4},{8,6},{10,8},{12,10},{14,12},{3,1},{5,3},{7,5},{... | collective-permute-start | bytes 258056 | tf_op jit(solution)/shard_map/ppermute | solution.py:34
  9.8 1.3 %collective-permute-done.1 = bf16[2,1,1,112,192]{4,3,2,1,0:T(8,128)(2,1)S(1)} collective-permute-done((bf16[2,1,1,112,192]{4,3,2,1,0:T(8,128)(2,1)S(1)}, bf16[2,1,1,112,192]{4,3,2,1,0:T(8,128)(2,1)S(1)}, u32[]{:S(2)}, u32[]{:S(2)}) %collective-permute-start.1) | collective-permute-done | bytes 86048 | tf_op jit(solution)/shard_map/ppermute | solution.py:33
  11.1 4.1 %collective-permute-done.2 = bf16[2,1,1,112,192]{4,3,2,1,0:T(8,128)(2,1)S(1)} collective-permute-done((bf16[2,1,1,112,192]{4,3,2,1,0:T(8,128)(2,1)S(1)}, bf16[2,1,1,112,192]{4,3,2,1,0:T(8,128)(2,1)S(1)}, u32[]{:S(2)}, u32[]{:S(2)}) %collective-permute-start.2) | collective-permute-done | bytes 86048 | tf_op jit(solution)/shard_map/ppermute | solution.py:34
  15.4 1.2 %pad_slice_fusion.16 = (bf16[1,2,112,192]{3,2,1,0:T(8,128)(2,1)S(1)}, bf16[1,2,112,192]{3,2,1,0:T(8,128)(2,1)S(1)}, bf16[1,2,112,192]{3,2,1,0:T(8,128)(2,1)S(1)}...) fusion(bf16[1,4,112,192]{3,2,1,0:T(8,128)(2,1)S(1)} %get-tuple-, ...), kind=kLoop, calls=%fused_computation.68 | loop fusion | bytes 2695168 | tf_op jit(solution)/shard_map/slice | solution.py:59
  16.8 5.4 %concatenate.13 = bf16[1,2,112,5184]{3,2,1,0:T(8,128)(2,1)} concatenate(bf16[1,2,112,192]{3,2,1,0:T(8,128)(2,1)S(1)} %pad.24, bf16[1,2,112,192]{3,2,1,0:T(8,128)(2,1)S(1)} %pad.25, bf16[1,2,112,192]{3,2,1,0:T(8,128)(2,1)S(1)} %pad.26, bf16[1,2,112,192]{3,2,1,0:T(8,128)(2,1)S(1)} %pad.24, bf16[1,2,112,192]{3,2,1,0:T(8,128)(2,1)S(1)} %pad.25, bf16[1,2,112,192]{3,2,1,0:T(8,128)(2,1)S(1)} %pad.26, ...), dimensions={3} | concatenate | bytes 4644864 | tf_op jit(solution)/shard_map/concatenate | solution.py:61
  22.3 2.5 %multiply_reduce_fusion.1 = (f32[2,112]{1,0:T(2,128)S(1)}, f32[2,112,192]{2,1,0:T(8,128)S(1)}) fusion(f32[192]{0:T(256)S(1)} %copy-done.10, bf16[5184,192,1]{1,0,2:T(8,128)(2,1)S(1)} %bitcast.82, bf16[1,2,112,5184]{3,2,1,0:T(8,128)(2,1)} %concatenate.13), kind=kOutput, calls=%fused_computation.55 | convolution fusion | flops 446035744 | bytes 4486784 | tf_op jit(solution)/shard_map/dot_general | solution.py:64
  27.1 4.3 %collective-permute-start.4 = (bf16[2,1,1,112,192]{4,3,2,1,0:T(8,128)(2,1)}, bf16[2,1,1,112,192]{4,3,2,1,0:T(8,128)(2,1)S(1)}, u32[]{:S(2)}, u32[]{:S(2)}) collective-permute-start(bf16[2,1,1,112,192]{4,3,2,1,0:T(8,128)(2,1)} %get-tuple-element.29), channel_id=1, source_target_pairs={{0,2},{2,4},{4,6},{6,8},{8,10},{10,12},{12,14},{1,3},{3,5},{5,7},{... | collective-permute-start | bytes 258056 | tf_op jit(solution)/shard_map/ppermute | solution.py:33
  31.5 1.3 %collective-permute-start.5 = (bf16[2,1,1,112,192]{4,3,2,1,0:T(8,128)(2,1)}, bf16[2,1,1,112,192]{4,3,2,1,0:T(8,128)(2,1)}, u32[]{:S(2)}, u32[]{:S(2)}) collective-permute-start(bf16[2,1,1,112,192]{4,3,2,1,0:T(8,128)(2,1)} %get-tuple-element.30), channel_id=1, source_target_pairs={{2,0},{4,2},{6,4},{8,6},{10,8},{12,10},{14,12},{3,1},{5,3},{7,5},{... | collective-permute-start | bytes 258056 | tf_op jit(solution)/shard_map/ppermute | solution.py:34
  32.9 1.6 %collective-permute-done.4 = bf16[2,1,1,112,192]{4,3,2,1,0:T(8,128)(2,1)S(1)} collective-permute-done((bf16[2,1,1,112,192]{4,3,2,1,0:T(8,128)(2,1)}, bf16[2,1,1,112,192]{4,3,2,1,0:T(8,128)(2,1)S(1)}, u32[]{:S(2)}, u32[]{:S(2)}) %collective-permute-start.4) | collective-permute-done | bytes 86048 | tf_op jit(solution)/shard_map/ppermute | solution.py:33
  34.5 4.1 %collective-permute-done.5 = bf16[2,1,1,112,192]{4,3,2,1,0:T(8,128)(2,1)} collective-permute-done((bf16[2,1,1,112,192]{4,3,2,1,0:T(8,128)(2,1)}, bf16[2,1,1,112,192]{4,3,2,1,0:T(8,128)(2,1)}, u32[]{:S(2)}, u32[]{:S(2)}) %collective-permute-start.5) | collective-permute-done | bytes 86048 | tf_op jit(solution)/shard_map/ppermute | solution.py:34
  41.5 5.4 %concatenate.15 = bf16[1,2,112,5184]{3,2,1,0:T(8,128)(2,1)} concatenate(bf16[1,2,112,192]{3,2,1,0:T(8,128)(2,1)S(1)} %pad.24, bf16[1,2,112,192]{3,2,1,0:T(8,128)(2,1)S(1)} %pad.25, bf16[1,2,112,192]{3,2,1,0:T(8,128)(2,1)S(1)} %pad.26, bf16[1,2,112,192]{3,2,1,0:T(8,128)(2,1)S(1)} %pad.24, bf16[1,2,112,192]{3,2,1,0:T(8,128)(2,1)S(1)} %pad.25, bf16[1,2,112,192]{3,2,1,0:T(8,128)(2,1)S(1)} %pad.26, ...), dimensions={3} | concatenate | bytes 4644864 | tf_op jit(solution)/shard_map/concatenate | solution.py:61
  47.0 3.4 %multiply_reduce_fusion = (f32[2,112]{1,0:T(2,128)S(1)}, f32[2,112,192]{2,1,0:T(8,128)S(1)}) fusion(f32[192]{0:T(256)S(1)} %copy-done.11, bf16[5184,192,1]{1,0,2:T(8,128)(2,1)} %bitcast.85, bf16[1,2,112,5184]{3,2,1,0:T(8,128)(2,1)} %concatenate.15, bf16[1,1,2,112,192]{4,3,2,1,0:T(8,128)(2,1)S(1)} %copy.16), kind=kOutput, calls=%fused_computation.53 | convolution fusion | flops 446121760 | bytes 4572800 | tf_op jit(solution)/shard_map/dot_general | solution.py:64
  52.2 1.7 %collective-permute-start.6 = (bf16[2,112,192]{2,1,0:T(8,128)(2,1)S(1)}, bf16[2,112,192]{2,1,0:T(8,128)(2,1)S(1)}, u32[]{:S(2)}, u32[]{:S(2)}) collective-permute-start(bf16[2,112,192]{2,1,0:T(8,128)(2,1)S(1)} %get-tuple-element.6), channel_id=1, source_target_pairs={{0,2},{2,4},{4,6},{6,8},{8,10},{10,12},{12,14},{14,0},{1,3},{3,5},... | collective-permute-start | bytes 258056 | tf_op jit(solution)/shard_map/ppermute | solution.py:15
  54.2 5.5 %collective-permute-done.6 = bf16[2,112,192]{2,1,0:T(8,128)(2,1)S(1)} collective-permute-done((bf16[2,112,192]{2,1,0:T(8,128)(2,1)S(1)}, bf16[2,112,192]{2,1,0:T(8,128)(2,1)S(1)}, u32[]{:S(2)}, u32[]{:S(2)}) %collective-permute-start.6) | collective-permute-done | bytes 86048 | tf_op jit(solution)/shard_map/ppermute | solution.py:15
  60.3 6.8 %collective-permute-done.7 = bf16[2,112,192]{2,1,0:T(8,128)(2,1)S(1)} collective-permute-done((bf16[2,112,192]{2,1,0:T(8,128)(2,1)S(1)}, bf16[2,112,192]{2,1,0:T(8,128)(2,1)S(1)}, u32[]{:S(2)}, u32[]{:S(2)}) %collective-permute-start.7) | collective-permute-done | bytes 86048 | tf_op jit(solution)/shard_map/ppermute | solution.py:15
  67.8 6.8 %collective-permute-done.8 = bf16[2,112,192]{2,1,0:T(8,128)(2,1)S(1)} collective-permute-done((bf16[2,112,192]{2,1,0:T(8,128)(2,1)S(1)}, bf16[2,112,192]{2,1,0:T(8,128)(2,1)S(1)}, u32[]{:S(2)}, u32[]{:S(2)}) %collective-permute-start.8) | collective-permute-done | bytes 86048 | tf_op jit(solution)/shard_map/ppermute | solution.py:15
  75.3 7.2 %collective-permute-done.9 = bf16[2,112,192]{2,1,0:T(8,128)(2,1)S(1)} collective-permute-done((bf16[2,112,192]{2,1,0:T(8,128)(2,1)S(1)}, bf16[2,112,192]{2,1,0:T(8,128)(2,1)S(1)}, u32[]{:S(2)}, u32[]{:S(2)}) %collective-permute-start.9) | collective-permute-done | bytes 86048 | tf_op jit(solution)/shard_map/ppermute | solution.py:15
  83.1 7.8 %collective-permute-done.10 = bf16[2,112,192]{2,1,0:T(8,128)(2,1)S(1)} collective-permute-done((bf16[2,112,192]{2,1,0:T(8,128)(2,1)S(1)}, bf16[2,112,192]{2,1,0:T(8,128)(2,1)S(1)}, u32[]{:S(2)}, u32[]{:S(2)}) %collective-permute-start.10) | collective-permute-done | bytes 86048 | tf_op jit(solution)/shard_map/ppermute | solution.py:15
  91.6 7.0 %collective-permute-done.11 = bf16[2,112,192]{2,1,0:T(8,128)(2,1)S(1)} collective-permute-done((bf16[2,112,192]{2,1,0:T(8,128)(2,1)S(1)}, bf16[2,112,192]{2,1,0:T(8,128)(2,1)S(1)}, u32[]{:S(2)}, u32[]{:S(2)}) %collective-permute-start.11) | collective-permute-done | bytes 86048 | tf_op jit(solution)/shard_map/ppermute | solution.py:15
  99.2 6.8 %collective-permute-done.12 = bf16[2,112,192]{2,1,0:T(8,128)(2,1)S(1)} collective-permute-done((bf16[2,112,192]{2,1,0:T(8,128)(2,1)S(1)}, bf16[2,112,192]{2,1,0:T(8,128)(2,1)S(1)}, u32[]{:S(2)}, u32[]{:S(2)}) %collective-permute-start.12) | collective-permute-done | bytes 86048 | tf_op jit(solution)/shard_map/ppermute | solution.py:15
  106.7 2.9 %fusion.45 = (f32[224]{0:T(256)S(1)}, f32[224,1792]{1,0:T(8,128)}) fusion(bf16[1792,192]{1,0:T(8,128)(2,1)} %bitcast.18, bf16[224,192]{1,0:T(8,128)(2,1)S(1)} %fusion.16, bf16[192,192]{1,0:T(8,128)(2,1)S(1)} %copy-done.1), kind=kOutput, calls=%fused_computation.103 | convolution fusion | flops 171142944 | bytes 2454400 | tf_op jit(solution)/shard_map/fqc,fkc->fqk/dot_general | solution.py:72
  109.7 1.8 %fusion.4 = f32[224]{0:T(256)S(1)} fusion(f32[224,1792]{1,0:T(8,128)} %get-tuple-element.58, f32[224]{0:T(256)S(1)} %broadcast_maximum_fusion), kind=kLoop, calls=%fused_computation.5 | loop fusion | flops 802592 | bytes 1607424 | tf_op jit(solution)/shard_map/reduce_sum | solution.py:75
  111.5 2.1 %fusion.18 = bf16[224,192]{1,0:T(8,128)(2,1)S(1)} fusion(bf16[1792,192]{1,0:T(8,128)(2,1)} %bitcast.18, f32[224,1792]{1,0:T(8,128)} %get-tuple-element.58, f32[224]{0:T(256)S(1)} %broadcast_maximum_fusion, f32[224]{0:T(256)S(1)} %fusion.4), kind=kOutput, calls=%fused_computation.18 | convolution fusion | flops 155029504 | bytes 2381568 | tf_op jit(solution)/shard_map/fqk,fkc->fqc/dot_general | solution.py:76
  (73 shorter events, 17.1 us)
Async XLA Ops:
  0.0 22.2 %copy-start = (bf16[3,3,3,192,192]{4,3,2,1,0:T(8,128)(2,1)S(1)}, bf16[3,3,3,192,192]{4,3,2,1,0:T(8,128)(2,1)}, u32[]{:S(2)}) copy-start(bf16[3,3,3,192,192]{4,3,2,1,0:T(8,128)(2,1)} %param.17) | copy-start | bytes 5971972
  2.1 1.5 %collective-permute-start = (bf16[1,2,112,192]{3,2,1,0:T(8,128)(2,1)S(1)}, bf16[1,2,112,192]{3,2,1,0:T(8,128)(2,1)S(1)}, u32[]{:S(2)}, u32[]{:S(2)}) collective-permute-start(bf16[1,2,112,192]{3,2,1,0:T(8,128)(2,1)S(1)} %fusion.32), channel_id=1, source_target_pairs={{1,0},{0,1},{3,2},{2,3},{5,4},{4,5},{7,6},{6,7},{9,8},{8,9},{11,10... | collective-permute-start | bytes 258056 | tf_op jit(solution)/shard_map/ppermute | solution.py:23
  3.7 7.5 %collective-permute-start.1 = (bf16[2,1,1,112,192]{4,3,2,1,0:T(8,128)(2,1)S(1)}, bf16[2,1,1,112,192]{4,3,2,1,0:T(8,128)(2,1)S(1)}, u32[]{:S(2)}, u32[]{:S(2)}) collective-permute-start(bf16[2,1,1,112,192]{4,3,2,1,0:T(8,128)(2,1)S(1)} %get-tuple-element.49), channel_id=1, source_target_pairs={{0,2},{2,4},{4,6},{6,8},{8,10},{10,12},{12,14},{1,3},{3,5},{5,7},{... | collective-permute-start | bytes 258056 | tf_op jit(solution)/shard_map/ppermute | solution.py:33
  8.4 6.8 %collective-permute-start.2 = (bf16[2,1,1,112,192]{4,3,2,1,0:T(8,128)(2,1)S(1)}, bf16[2,1,1,112,192]{4,3,2,1,0:T(8,128)(2,1)S(1)}, u32[]{:S(2)}, u32[]{:S(2)}) collective-permute-start(bf16[2,1,1,112,192]{4,3,2,1,0:T(8,128)(2,1)S(1)} %get-tuple-element.50), channel_id=1, source_target_pairs={{2,0},{4,2},{6,4},{8,6},{10,8},{12,10},{14,12},{3,1},{5,3},{7,5},{... | collective-permute-start | bytes 258056 | tf_op jit(solution)/shard_map/ppermute | solution.py:34
  16.8 5.5 %copy-start.10 = (f32[192]{0:T(256)S(1)}, f32[192]{0:T(256)}, u32[]{:S(2)}) copy-start(f32[192]{0:T(256)} %param.18) | copy-start | bytes 2308
  25.0 1.4 %collective-permute-start.3 = (bf16[1,2,112,192]{3,2,1,0:T(8,128)(2,1)S(1)}, bf16[1,2,112,192]{3,2,1,0:T(8,128)(2,1)S(1)}, u32[]{:S(2)}, u32[]{:S(2)}) collective-permute-start(bf16[1,2,112,192]{3,2,1,0:T(8,128)(2,1)S(1)} %fusion.57), channel_id=1, source_target_pairs={{1,0},{0,1},{3,2},{2,3},{5,4},{4,5},{7,6},{6,7},{9,8},{8,9},{11,10... | collective-permute-start | bytes 258056 | tf_op jit(solution)/shard_map/ppermute | solution.py:23
  27.1 7.4 %collective-permute-start.4 = (bf16[2,1,1,112,192]{4,3,2,1,0:T(8,128)(2,1)}, bf16[2,1,1,112,192]{4,3,2,1,0:T(8,128)(2,1)S(1)}, u32[]{:S(2)}, u32[]{:S(2)}) collective-permute-start(bf16[2,1,1,112,192]{4,3,2,1,0:T(8,128)(2,1)} %get-tuple-element.29), channel_id=1, source_target_pairs={{0,2},{2,4},{4,6},{6,8},{8,10},{10,12},{12,14},{1,3},{3,5},{5,7},{... | collective-permute-start | bytes 258056 | tf_op jit(solution)/shard_map/ppermute | solution.py:33
  31.5 7.1 %collective-permute-start.5 = (bf16[2,1,1,112,192]{4,3,2,1,0:T(8,128)(2,1)}, bf16[2,1,1,112,192]{4,3,2,1,0:T(8,128)(2,1)}, u32[]{:S(2)}, u32[]{:S(2)}) collective-permute-start(bf16[2,1,1,112,192]{4,3,2,1,0:T(8,128)(2,1)} %get-tuple-element.30), channel_id=1, source_target_pairs={{2,0},{4,2},{6,4},{8,6},{10,8},{12,10},{14,12},{3,1},{5,3},{7,5},{... | collective-permute-start | bytes 258056 | tf_op jit(solution)/shard_map/ppermute | solution.py:34
  41.5 5.4 %copy-start.11 = (f32[192]{0:T(256)S(1)}, f32[192]{0:T(256)}, u32[]{:S(2)}) copy-start(f32[192]{0:T(256)} %param.21) | copy-start | bytes 2308
  47.0 4.5 %copy-start.6 = (f32[192]{0:T(256)S(1)}, f32[192]{0:T(256)}, u32[]{:S(2)}) copy-start(f32[192]{0:T(256)} %param.22) | copy-start | bytes 2308
  47.0 6.9 %copy-start.2 = (bf16[192,192]{1,0:T(8,128)(2,1)S(1)}, bf16[192,192]{1,0:T(8,128)(2,1)}, u32[]{:S(2)}) copy-start(bf16[192,192]{1,0:T(8,128)(2,1)} %param.23) | copy-start | bytes 221188
  47.0 6.9 %copy-start.7 = (f32[192]{0:T(256)S(1)}, f32[192]{0:T(256)}, u32[]{:S(2)}) copy-start(f32[192]{0:T(256)} %param.24) | copy-start | bytes 2308
  50.4 56.3 %copy-start.1 = (bf16[192,192]{1,0:T(8,128)(2,1)S(1)}, bf16[192,192]{1,0:T(8,128)(2,1)}, u32[]{:S(2)}) copy-start(bf16[192,192]{1,0:T(8,128)(2,1)} %param.25) | copy-start | bytes 221188
  52.2 7.5 %collective-permute-start.6 = (bf16[2,112,192]{2,1,0:T(8,128)(2,1)S(1)}, bf16[2,112,192]{2,1,0:T(8,128)(2,1)S(1)}, u32[]{:S(2)}, u32[]{:S(2)}) collective-permute-start(bf16[2,112,192]{2,1,0:T(8,128)(2,1)S(1)} %get-tuple-element.6), channel_id=1, source_target_pairs={{0,2},{2,4},{4,6},{6,8},{8,10},{10,12},{12,14},{14,0},{1,3},{3,5},... | collective-permute-start | bytes 258056 | tf_op jit(solution)/shard_map/ppermute | solution.py:15
  59.7 7.5 %collective-permute-start.7 = (bf16[2,112,192]{2,1,0:T(8,128)(2,1)S(1)}, bf16[2,112,192]{2,1,0:T(8,128)(2,1)S(1)}, u32[]{:S(2)}, u32[]{:S(2)}) collective-permute-start(bf16[2,112,192]{2,1,0:T(8,128)(2,1)S(1)} %collective-permute-done.6), channel_id=1, source_target_pairs={{0,2},{2,4},{4,6},{6,8},{8,10},{10,12},{12,14},{14,0},{1,3},{3,5},... | collective-permute-start | bytes 258056 | tf_op jit(solution)/shard_map/ppermute | solution.py:15
  67.2 7.5 %collective-permute-start.8 = (bf16[2,112,192]{2,1,0:T(8,128)(2,1)S(1)}, bf16[2,112,192]{2,1,0:T(8,128)(2,1)S(1)}, u32[]{:S(2)}, u32[]{:S(2)}) collective-permute-start(bf16[2,112,192]{2,1,0:T(8,128)(2,1)S(1)} %collective-permute-done.7), channel_id=1, source_target_pairs={{0,2},{2,4},{4,6},{6,8},{8,10},{10,12},{12,14},{14,0},{1,3},{3,5},... | collective-permute-start | bytes 258056 | tf_op jit(solution)/shard_map/ppermute | solution.py:15
  74.7 7.8 %collective-permute-start.9 = (bf16[2,112,192]{2,1,0:T(8,128)(2,1)S(1)}, bf16[2,112,192]{2,1,0:T(8,128)(2,1)S(1)}, u32[]{:S(2)}, u32[]{:S(2)}) collective-permute-start(bf16[2,112,192]{2,1,0:T(8,128)(2,1)S(1)} %collective-permute-done.8), channel_id=1, source_target_pairs={{0,2},{2,4},{4,6},{6,8},{8,10},{10,12},{12,14},{14,0},{1,3},{3,5},... | collective-permute-start | bytes 258056 | tf_op jit(solution)/shard_map/ppermute | solution.py:15
  82.5 8.5 %collective-permute-start.10 = (bf16[2,112,192]{2,1,0:T(8,128)(2,1)S(1)}, bf16[2,112,192]{2,1,0:T(8,128)(2,1)S(1)}, u32[]{:S(2)}, u32[]{:S(2)}) collective-permute-start(bf16[2,112,192]{2,1,0:T(8,128)(2,1)S(1)} %collective-permute-done.9), channel_id=1, source_target_pairs={{0,2},{2,4},{4,6},{6,8},{8,10},{10,12},{12,14},{14,0},{1,3},{3,5},... | collective-permute-start | bytes 258056 | tf_op jit(solution)/shard_map/ppermute | solution.py:15
  90.9 7.6 %collective-permute-start.11 = (bf16[2,112,192]{2,1,0:T(8,128)(2,1)S(1)}, bf16[2,112,192]{2,1,0:T(8,128)(2,1)S(1)}, u32[]{:S(2)}, u32[]{:S(2)}) collective-permute-start(bf16[2,112,192]{2,1,0:T(8,128)(2,1)S(1)} %collective-permute-done.10), channel_id=1, source_target_pairs={{0,2},{2,4},{4,6},{6,8},{8,10},{10,12},{12,14},{14,0},{1,3},{3,5},... | collective-permute-start | bytes 258056 | tf_op jit(solution)/shard_map/ppermute | solution.py:15
  98.6 7.5 %collective-permute-start.12 = (bf16[2,112,192]{2,1,0:T(8,128)(2,1)S(1)}, bf16[2,112,192]{2,1,0:T(8,128)(2,1)S(1)}, u32[]{:S(2)}, u32[]{:S(2)}) collective-permute-start(bf16[2,112,192]{2,1,0:T(8,128)(2,1)S(1)} %collective-permute-done.11), channel_id=1, source_target_pairs={{0,2},{2,4},{4,6},{6,8},{8,10},{10,12},{12,14},{14,0},{1,3},{3,5},... | collective-permute-start | bytes 258056 | tf_op jit(solution)/shard_map/ppermute | solution.py:15
  109.7 3.9 %copy-start.3 = (bf16[192,192]{1,0:T(8,128)(2,1)S(1)}, bf16[192,192]{1,0:T(8,128)(2,1)}, u32[]{:S(2)}) copy-start(bf16[192,192]{1,0:T(8,128)(2,1)} %param.28) | copy-start | bytes 221188
  109.7 4.0 %copy-start.4 = (bf16[192,192]{1,0:T(8,128)(2,1)S(1)}, bf16[192,192]{1,0:T(8,128)(2,1)}, u32[]{:S(2)}) copy-start(bf16[192,192]{1,0:T(8,128)(2,1)} %param.26) | copy-start | bytes 221188
  109.7 4.0 %copy-start.8 = (f32[192]{0:T(256)S(1)}, f32[192]{0:T(256)}, u32[]{:S(2)}) copy-start(f32[192]{0:T(256)} %param.27) | copy-start | bytes 2308
  109.7 4.0 %copy-start.9 = (f32[192]{0:T(256)S(1)}, f32[192]{0:T(256)}, u32[]{:S(2)}) copy-start(f32[192]{0:T(256)} %param.29) | copy-start | bytes 2308
  (1 other events, 2.6 us)
